TPU v7x, 32 devices: a whole 2x2x4 slice. The times are simulated.
32 devices in a mesh: groups: 2 (over y), chan: 4 (over z), tm: 4 (over x, core).
Axes of the slice: x: 2, y: 2, z: 4, core: 2. Of those that a mesh axis runs over, the one named last changes fastest.
Arguments:
- raw: bfloat16 [8192, 2048], P(('groups', 'chan'), 'tm'), parts along dimension 0, may hold values from -20 to 20
- send_blocks: int32 [4, 4, 4, 1], P('chan', 'tm'), may hold values from 0 to 1, as said below
- pair_count: int32 [4, 4, 4], P('chan', 'tm'), may hold values from 0 to 1, as said below
Outputs:
- xspec: bfloat16 [8, 4, 4, 1, 2, 2, 128, 128], P(('groups', 'chan'), 'tm'), parts along dimension 0
There are 2 independent parts, one for each index of `groups`. A program takes and returns all parts, laid end to end along the dimension named above; an argument that names none is the same for every part. Nothing has to cross between parts.
Inputs may be any that keep to these rules, and one draw needn't show every extreme that they name: Each list send_blocks[p, t, c, :] names 1 distinct local blocks of device (p, t). pair_count[c, t, c] is 0; pair_count[c, t, p] is 1 where p and c differ by one; in every index t of tm some owner has 1 from every other source.
All inputs are finite; a program needn't handle non-finite values.
Results may differ from a plain program's by a relative error of at most 0.0066.
Values may be sent and summed in bfloat16 or wider, within the bound.
No kernel may reach another device: no remote copies, remote signals or barrier semaphores. Data moves between devices by JAX's collectives and lax.ppermute only.
A program may use at most 192 MiB of HBM per device.

v0:
```python
import math
import jax
import jax.numpy as jnp
import numpy as np
from jax import lax
from jax.sharding import PartitionSpec as P

BLOCK = 128
NT = 2048
F0 = 128
NBAND = 512
SUBW = 64
RAD = 15


def sinc_value(arg):
    if arg == 0:
        return 1.0
    return math.sin(math.pi * arg) / (math.pi * arg)


def filter_taps():
    low = F0 / NT
    high = (F0 + NBAND) / NT
    taps = []
    for offset in range(-RAD, RAD + 1):
        value = 2.0 * high * sinc_value(2.0 * high * offset) - 2.0 * low * sinc_value(
            2.0 * low * offset
        )
        value = value * (0.5 + 0.5 * math.cos(math.pi * offset / (RAD + 1)))
        taps.append(value)
    return taps


def dft_table():
    samples = np.arange(NT)[:, None]
    freqs = np.arange(F0, F0 + NBAND)[None, :]
    phase = samples * freqs % NT
    angle = 2.0 * np.pi * phase / NT
    return np.concatenate([np.cos(angle), -np.sin(angle)], axis=1)


def band_filter(slab):
    taps = filter_taps()
    signal = slab.astype(jnp.float32)
    total = jnp.zeros(signal.shape, jnp.float32)
    for index in range(2 * RAD + 1):
        total = total + jnp.float32(taps[index]) * jnp.roll(signal, index - RAD, axis=1)
    return total.astype(jnp.bfloat16)


def whiten(spectrum):
    rows = spectrum.shape[0]
    real_part = spectrum[:, :NBAND].reshape(rows, NBAND // SUBW, SUBW)
    imag_part = spectrum[:, NBAND:].reshape(rows, NBAND // SUBW, SUBW)
    power = jnp.mean(real_part * real_part + imag_part * imag_part, axis=2, keepdims=True)
    level = 1.0 / jnp.sqrt(power + 1e-06)
    out = jnp.concatenate(
        [(real_part * level).reshape(rows, NBAND), (imag_part * level).reshape(rows, NBAND)], axis=1
    )
    return out.astype(jnp.bfloat16)


def local(raw, send_blocks, pair_count):
    rows = lax.all_to_all(raw, "tm", split_axis=0, concat_axis=1, tiled=True)
    table = jnp.asarray(dft_table(), dtype=jnp.bfloat16)
    spectrum = jnp.dot(band_filter(rows), table, preferred_element_type=jnp.float32)
    blocks = rows.shape[0] // BLOCK
    whitened = whiten(spectrum).reshape(blocks, BLOCK, 2 * NBAND)
    peers = lax.axis_size("chan")
    width = send_blocks.shape[3]
    every, lists_all = (
        lax.all_gather(whitened, "chan", axis=0, tiled=True),
        lax.all_gather(send_blocks.astype(jnp.bfloat16), "chan", axis=0, tiled=True),
    )
    mine = lax.axis_index("chan")
    column = lax.dynamic_index_in_dim(lists_all[:, 0], mine, axis=1, keepdims=False)
    flat_ids = jnp.arange(peers, dtype=jnp.int32)[:, None] * blocks + column.astype(jnp.int32)
    picked = every[flat_ids]
    turned = jnp.concatenate([whitened[..., NBAND:], -whitened[..., :NBAND]], axis=-1)
    paired = jnp.stack([whitened, turned], axis=1)
    result = jnp.einsum("lrif,pkjf->pklrij", paired, picked, preferred_element_type=jnp.float32)
    result = result * (1.0 / math.sqrt(NBAND))
    live = jnp.arange(width, dtype=jnp.int32)[None, :] < pair_count[0, 0][:, None]
    result = jnp.where(live[:, :, None, None, None, None], result, 0.0)
    return result.astype(jnp.bfloat16)[None, None]


def solution(mesh):
    return jax.shard_map(
        local,
        mesh=mesh,
        in_specs=(P(("groups", "chan"), "tm"), P("chan", "tm", None, None), P("chan", "tm", None)),
        out_specs=P(("groups", "chan"), "tm", None, None, None, None, None, None),
        check_vma=False,
    )
```

profile of v0, /device:TPU:0, one launch (start us, length us, event | category | flops | bytes accessed | tf_op | source)
XLA Modules:
  0.0 150.9 jit_solution(17581047669316288742)
XLA Ops:
  6.5 18.7 %all_to_all.13 = bf16[4,256,512]{2,1,0:T(8,128)(2,1)S(1)} all-to-all(bf16[4,256,512]{2,1,0:T(8,128)(2,1)} %bitcast.81), channel_id=1, replica_groups=mesh['groups'=2,'chan'=4,'tm'=4] {'tm'}, dimensions={0} | all-to-all | bytes 2097152 | tf_op jit(solution)/shard_map/all_to_all | solution.py:65
  25.2 1.6 %convert_bitcast_fusion = f32[256,4,512]{2,0,1:T(8,128)} fusion(bf16[4,256,512]{2,1,0:T(8,128)(2,1)S(1)} %all_to_all.13), kind=kLoop, calls=%fused_computation.62 | loop fusion | flops 524288 | bytes 3145728 | tf_op jit(solution)/shard_map/convert_element_type | solution.py:45
  26.8 1.9 %copy.21 = f32[256,4,512]{0,2,1:T(8,128)S(1)} copy(f32[256,4,512]{2,0,1:T(8,128)} %convert_bitcast_fusion) | data formatting | bytes 4194304 | tf_op jit(solution)/shard_map/convert_element_type | solution.py:45
  28.8 2.3 %fusion.76 = (f32[256,2041]{0,1:T(8,128)}, f32[256,2041]{0,1:T(8,128)}) fusion(f32[256,2048]{0,1:T(8,128)S(1)} %bitcast.46), kind=kLoop, calls=%fused_computation.121 | loop fusion | bytes 8359936 | tf_op jit(solution)/shard_map/jit(_roll_static)/slice | solution.py:48
  31.1 2.3 %fusion.78 = (f32[256,2042]{0,1:T(8,128)}, f32[256,2042]{0,1:T(8,128)}) fusion(f32[256,2048]{0,1:T(8,128)S(1)} %bitcast.47), kind=kLoop, calls=%fused_computation.123 | loop fusion | bytes 8364032 | tf_op jit(solution)/shard_map/jit(_roll_static)/slice | solution.py:48
  33.4 2.3 %fusion.80 = (f32[256,2043]{0,1:T(8,128)}, f32[256,2043]{0,1:T(8,128)}) fusion(f32[256,2048]{0,1:T(8,128)S(1)} %bitcast.48), kind=kLoop, calls=%fused_computation.125 | loop fusion | bytes 8368128 | tf_op jit(solution)/shard_map/jit(_roll_static)/slice | solution.py:48
  35.7 2.3 %fusion.82 = (f32[256,2044]{0,1:T(8,128)}, f32[256,2044]{0,1:T(8,128)}) fusion(f32[256,2048]{0,1:T(8,128)S(1)} %bitcast.49), kind=kLoop, calls=%fused_computation.127 | loop fusion | bytes 8372224 | tf_op jit(solution)/shard_map/jit(_roll_static)/slice | solution.py:48
  38.0 2.3 %fusion.84 = (f32[256,2045]{0,1:T(8,128)}, f32[256,2045]{0,1:T(8,128)}) fusion(f32[256,2048]{0,1:T(8,128)S(1)} %bitcast.50), kind=kLoop, calls=%fused_computation.129 | loop fusion | bytes 8376320 | tf_op jit(solution)/shard_map/jit(_roll_static)/slice | solution.py:48
  40.3 2.3 %fusion.86 = (f32[256,2046]{0,1:T(8,128)}, f32[256,2046]{0,1:T(8,128)}) fusion(f32[256,2048]{0,1:T(8,128)S(1)} %bitcast.51), kind=kLoop, calls=%fused_computation.131 | loop fusion | bytes 8380416 | tf_op jit(solution)/shard_map/jit(_roll_static)/slice | solution.py:48
  42.6 2.3 %fusion.88 = (f32[256,2047]{0,1:T(8,128)}, f32[256,2047]{0,1:T(8,128)}) fusion(f32[256,2048]{0,1:T(8,128)S(1)} %bitcast.52), kind=kLoop, calls=%fused_computation.133 | loop fusion | bytes 8384512 | tf_op jit(solution)/shard_map/jit(_roll_static)/slice | solution.py:48
  44.9 2.3 %fusion.62 = (f32[256,2034]{0,1:T(8,128)}, f32[256,2034]{0,1:T(8,128)}) fusion(f32[256,2048]{0,1:T(8,128)S(1)} %bitcast.53), kind=kLoop, calls=%fused_computation.107 | loop fusion | bytes 8331264 | tf_op jit(solution)/shard_map/jit(_roll_static)/slice | solution.py:48
  47.2 2.3 %fusion.64 = (f32[256,2035]{0,1:T(8,128)}, f32[256,2035]{0,1:T(8,128)}) fusion(f32[256,2048]{0,1:T(8,128)S(1)} %bitcast.54), kind=kLoop, calls=%fused_computation.109 | loop fusion | bytes 8335360 | tf_op jit(solution)/shard_map/jit(_roll_static)/slice | solution.py:48
  49.5 2.3 %fusion.66 = (f32[256,2036]{0,1:T(8,128)}, f32[256,2036]{0,1:T(8,128)}) fusion(f32[256,2048]{0,1:T(8,128)S(1)} %bitcast.55), kind=kLoop, calls=%fused_computation.111 | loop fusion | bytes 8339456 | tf_op jit(solution)/shard_map/jit(_roll_static)/slice | solution.py:48
  51.8 2.3 %fusion.68 = (f32[256,2037]{0,1:T(8,128)}, f32[256,2037]{0,1:T(8,128)}) fusion(f32[256,2048]{0,1:T(8,128)S(1)} %bitcast.56), kind=kLoop, calls=%fused_computation.113 | loop fusion | bytes 8343552 | tf_op jit(solution)/shard_map/jit(_roll_static)/slice | solution.py:48
  54.1 2.3 %fusion.70 = (f32[256,2038]{0,1:T(8,128)}, f32[256,2038]{0,1:T(8,128)}) fusion(f32[256,2048]{0,1:T(8,128)S(1)} %bitcast.57), kind=kLoop, calls=%fused_computation.115 | loop fusion | bytes 8347648 | tf_op jit(solution)/shard_map/jit(_roll_static)/slice | solution.py:48
  56.3 2.3 %fusion.72 = (f32[256,2039]{0,1:T(8,128)}, f32[256,2039]{0,1:T(8,128)}) fusion(f32[256,2048]{0,1:T(8,128)S(1)} %bitcast.58), kind=kLoop, calls=%fused_computation.117 | loop fusion | bytes 8351744 | tf_op jit(solution)/shard_map/jit(_roll_static)/slice | solution.py:48
  58.6 2.2 %fusion.74 = (f32[256,2040]{0,1:T(8,128)}, f32[256,2040]{0,1:T(8,128)}) fusion(f32[256,2048]{0,1:T(8,128)S(1)} %bitcast.59), kind=kLoop, calls=%fused_computation.119 | loop fusion | bytes 8355840 | tf_op jit(solution)/shard_map/jit(_roll_static)/slice | solution.py:48
  60.8 2.3 %fusion.60 = (f32[256,2033]{0,1:T(8,128)}, f32[256,2033]{0,1:T(8,128)}) fusion(f32[256,2048]{0,1:T(8,128)S(1)} %bitcast.60), kind=kLoop, calls=%fused_computation.105 | loop fusion | bytes 8327168 | tf_op jit(solution)/shard_map/jit(_roll_static)/slice | solution.py:48
  63.3 27.8 %fusion.40 = f32[256,1024]{1,0:T(8,128)S(1)} fusion(bf16[2048,1024]{1,0:T(8,128)(2,1)} %constant.58.clone, f32[256,2038]{0,1:T(8,128)} %get-tuple-element.26, f32[256,10]{0,1:T(8,128)S(1)} %get-tuple-element.28, f32[256,2037]{0,1:T(8,128)} %get-tuple-element.22, f32[256,11]{0,1:T(8,128)S(1)} %get-tuple-element.24, f32[256,2036]{0,1:T(8,128)} %get-tuple-element.18, ...), kind=kOutput, calls=%fused_computation.74 | convolution fusion | flops 1121976320 | bytes 70254592 | tf_op jit(solution)/shard_map/dot_general | solution.py:67
  91.1 0.1 multiply_add_fusion
  91.2 0.2 copy.22
  91.6 0.2 copy.23
  91.8 0.0 copy-start
  91.8 0.2 multiply_convert_fusion
  92.0 0.9 pad_maximum_fusion
  92.9 0.0 all-gather.2.cloned.1.call-update
  93.0 11.8 %all_gather.7 = bf16[4,1,4,1]{2,3,1,0:T(2,128)(2,1)S(1)} all-gather(bf16[1,1,4,1]{2,3,1,0:T(2,128)(2,1)S(1)} %convert_element_type.49), channel_id=1, replica_groups=mesh['groups'=2,'chan'=4,'tm'=4] {'chan'}, dimensions={0}, use_global_device_ids=true | all-gather | bytes 40 | tf_op jit(solution)/shard_map/all_gather | solution.py:74
  104.8 0.2 convert_reduce_fusion
  105.1 35.0 %all-gather.2.cloned.1.call-done = bf16[8,128,1024]{2,1,0:T(8,128)(2,1)} async-done(((bf16[2,128,1024]{2,1,0:T(8,128)(2,1)}), bf16[8,128,1024]{2,1,0:T(8,128)(2,1)}) %all-gather.2.cloned.1.call-update) | async-done | bytes 2097168 | tf_op jit(solution)/shard_map/all_gather | solution.py:73
  140.1 2.2 %gather_fusion = bf16[4,128,1024]{2,1,0:T(8,128)(2,1)S(1)} fusion(bf16[8,128,1024]{2,1,0:T(8,128)(2,1)} %all-gather.2.cloned.1.call-done, s32[1024]{0:T(1024)S(1)} %pad_clamp_fusion), kind=kCustom, calls=%fused_computation | custom fusion | bytes 2097168 | tf_op jit(solution)/shard_map/gather | solution.py:79
  142.3 0.8 fusion.34
  143.1 1.0 copy.27
  (27 shorter events, 0.3 us)
Async XLA Ops:
  6.5 133.6 %all-gather.2.cloned.1.call-start = ((), (), s32[]{:S(2)}) async-start(), calls=%async_computation.1 | async-start | bytes 2621440 | tf_op jit(solution)/shard_map/all_gather | solution.py:73
  91.8 1.2 copy-start
  91.8 13.3 %copy-start.1 = (s32[1,1,4]{2,1,0:T(1,128)S(1)}, s32[1,1,4]{2,1,0:T(1,128)}, u32[]{:S(2)}) copy-start(s32[1,1,4]{2,1,0:T(1,128)} %param.6) | copy-start | bytes 52
Sparse Core Ops, SparseCore 0:
  93.1 46.9 all-gather.1
where the time goes:
time: 151 us
  local copies, waits for them, and re-layouts  40 us (26%)
  waiting for transfers between devices  35 us (23%)
  blocking collectives  30.5 us (20%)
  matrix products  28.6 us (19%)
  between operations  13.7 us (9%)
  other arithmetic  3.18 us (2%)
    all_gather x1, waiting for transfers between devices, local(): lax.all_gather(whitened, 'chan', axis=0, tiled=True)  35 us
    slice x30, local copies, waits for them, and re-layouts, band_filter(): jnp.roll(signal, index - RAD, axis=1)  34.4 us
    dot_general x1, matrix products, local(): jnp.dot(band_filter(rows), table, preferred_element_type=jnp.float32)  27.8 us
    all_to_all x1, blocking collectives, local(): rows = lax.all_to_all(raw, 'tm', split_axis=0, concat_axis=1, tiled=True)  18.7 us
    all_gather x1, blocking collectives, local(): lax.all_gather(send_blocks.astype(jnp.bfloat16), 'chan', axis=0, tiled=True)  11.8 us
  transfers between devices with their start and end apart: 1, of which 1 were waited for; matrix products, arithmetic and copies ran while one was open for 0% of the time, Pallas kernels for 0%

commit v1 on v0

--- a/solution.py
+++ b/solution.py
@@ -11,6 +11,28 @@
 NBAND = 512
 SUBW = 64
 RAD = 15
+
+
+def laid_out(blocks, dim):
+    blocks = jnp.moveaxis(blocks, 0, dim)
+    shape = blocks.shape
+    return blocks.reshape(*shape[:dim], shape[dim] * shape[dim + 1], *shape[dim + 2 :])
+
+
+def ring_gather(x, axis, dim):
+    size = lax.axis_size(axis)
+    pairs = [(i, (i + 1) % size) for i in range(size)]
+    back = [(b, a) for a, b in pairs]
+    lower, upper = ([], [])
+    for step in range(size - 1):
+        if step % 2 == 0:
+            lower.append(lax.ppermute(lower[-1] if lower else x, axis, pairs))
+        else:
+            upper.append(lax.ppermute(upper[-1] if upper else x, axis, back))
+    tiles = jnp.stack([*lower[::-1], x, *upper])
+    shift = lax.axis_index(axis) - len(lower)
+    tiles = tiles[(jnp.arange(size) - shift) % size]
+    return laid_out(tiles, dim)
 
 
 def sinc_value(arg):
@@ -70,7 +92,7 @@
     peers = lax.axis_size("chan")
     width = send_blocks.shape[3]
     every, lists_all = (
-        lax.all_gather(whitened, "chan", axis=0, tiled=True),
+        ring_gather(whitened, "chan", 0),
         lax.all_gather(send_blocks.astype(jnp.bfloat16), "chan", axis=0, tiled=True),
     )
     mine = lax.axis_index("chan")

time: 151 us -> 136 us (0.901)
  waiting for transfers between devices: 35 us -> 20.6 us
  between operations: 13.7 us -> 0.28 us
  blocking collectives: 30.5 us -> 35.6 us
  starting transfers between devices: 0.01 us -> 4.42 us
  local copies, waits for them, and re-layouts: 40 us -> 42.1 us
    all_gather x1 -> x0, waiting for transfers between devices: 35 us -> none  [local(): lax.all_gather(whitened, 'chan', axis=0, tiled=True)]
    ppermute x0 -> x3, waiting for transfers between devices: none -> 20.6 us  [the longest x1 20.6 us: ring_gather(): upper.append(lax.ppermute(upper[-1] if upper else x, axis, back))]
    all_gather x1, blocking collectives: 11.8 us -> 16.9 us  [local(): lax.all_gather(send_blocks.astype(jnp.bfloat16), 'chan', axis=0, tiled=True)]
    ppermute x0 -> x3, starting transfers between devices: none -> 4.42 us  [the longest x2 3.92 us: ring_gather(): lower.append(lax.ppermute(lower[-1] if lower else x, axis, pairs))]
    gather x0 -> x1, local copies, waits for them, and re-layouts: none -> 2.04 us  [ring_gather(): tiles = tiles[(jnp.arange(size) - shift) % size]]
  transfers between devices with their start and end apart: 1 -> 3, of which waited for: 1 -> 1; matrix products, arithmetic and copies ran while one was open for 0% -> 0% of each run, Pallas kernels for 0% -> 0%
where the time goes in v1:
time: 136 us; the launch traced here: 135 us
  local copies, waits for them, and re-layouts  42.1 us (31%)
  blocking collectives  35.6 us (26%)
  matrix products  28.7 us (21%)
  waiting for transfers between devices  20.6 us (15%)
  starting transfers between devices  4.42 us (3%)
  other arithmetic  3.65 us (3%)
    slice x30, local copies, waits for them, and re-layouts, band_filter(): jnp.roll(signal, index - RAD, axis=1)  34.5 us
    dot_general x1, matrix products, local(): jnp.dot(band_filter(rows), table, preferred_element_type=jnp.float32)  27.9 us
    ppermute x1, waiting for transfers between devices, ring_gather(): upper.append(lax.ppermute(upper[-1] if upper else x, axis, back))  20.6 us
    all_to_all x1, blocking collectives, local(): rows = lax.all_to_all(raw, 'tm', split_axis=0, concat_axis=1, tiled=True)  18.7 us
    all_gather x1, blocking collectives, local(): lax.all_gather(send_blocks.astype(jnp.bfloat16), 'chan', axis=0, tiled=True)  16.9 us
    ppermute x2, starting transfers between devices, ring_gather(): lower.append(lax.ppermute(lower[-1] if lower else x, axis, pairs))  3.92 us
  transfers between devices with their start and end apart: 3, of which 1 were waited for; matrix products, arithmetic and copies ran while one was open for 0% of the time, Pallas kernels for 0%

profile of v1, /device:TPU:0, one launch (start us, length us, event | category | flops | bytes accessed | tf_op | source)
XLA Modules:
  0.0 135.3 jit_solution(7929040753597264441)
XLA Ops:
  0.0 18.7 %all_to_all.13 = bf16[4,256,512]{2,1,0:T(8,128)(2,1)S(1)} all-to-all(bf16[4,256,512]{2,1,0:T(8,128)(2,1)} %bitcast.94), channel_id=1, replica_groups=mesh['groups'=2,'chan'=4,'tm'=4] {'tm'}, dimensions={0} | all-to-all | bytes 2097152 | tf_op jit(solution)/shard_map/all_to_all | solution.py:87
  18.7 1.7 %convert_bitcast_fusion = f32[256,4,512]{2,0,1:T(8,128)} fusion(bf16[4,256,512]{2,1,0:T(8,128)(2,1)S(1)} %all_to_all.13), kind=kLoop, calls=%fused_computation.64 | loop fusion | flops 524288 | bytes 3145728 | tf_op jit(solution)/shard_map/convert_element_type | solution.py:67
  20.3 1.9 %copy.21 = f32[256,4,512]{0,2,1:T(8,128)S(1)} copy(f32[256,4,512]{2,0,1:T(8,128)} %convert_bitcast_fusion) | data formatting | bytes 4194304 | tf_op jit(solution)/shard_map/convert_element_type | solution.py:67
  22.2 2.3 %fusion.78 = (f32[256,2041]{0,1:T(8,128)}, f32[256,2041]{0,1:T(8,128)}) fusion(f32[256,2048]{0,1:T(8,128)S(1)} %bitcast.54), kind=kLoop, calls=%fused_computation.130 | loop fusion | bytes 8359936 | tf_op jit(solution)/shard_map/jit(_roll_static)/slice | solution.py:70
  24.6 2.3 %fusion.80 = (f32[256,2042]{0,1:T(8,128)}, f32[256,2042]{0,1:T(8,128)}) fusion(f32[256,2048]{0,1:T(8,128)S(1)} %bitcast.55), kind=kLoop, calls=%fused_computation.132 | loop fusion | bytes 8364032 | tf_op jit(solution)/shard_map/jit(_roll_static)/slice | solution.py:70
  26.9 2.3 %fusion.82 = (f32[256,2043]{0,1:T(8,128)}, f32[256,2043]{0,1:T(8,128)}) fusion(f32[256,2048]{0,1:T(8,128)S(1)} %bitcast.56), kind=kLoop, calls=%fused_computation.134 | loop fusion | bytes 8368128 | tf_op jit(solution)/shard_map/jit(_roll_static)/slice | solution.py:70
  29.2 2.3 %fusion.84 = (f32[256,2044]{0,1:T(8,128)}, f32[256,2044]{0,1:T(8,128)}) fusion(f32[256,2048]{0,1:T(8,128)S(1)} %bitcast.57), kind=kLoop, calls=%fused_computation.136 | loop fusion | bytes 8372224 | tf_op jit(solution)/shard_map/jit(_roll_static)/slice | solution.py:70
  31.5 2.3 %fusion.86 = (f32[256,2045]{0,1:T(8,128)}, f32[256,2045]{0,1:T(8,128)}) fusion(f32[256,2048]{0,1:T(8,128)S(1)} %bitcast.58), kind=kLoop, calls=%fused_computation.138 | loop fusion | bytes 8376320 | tf_op jit(solution)/shard_map/jit(_roll_static)/slice | solution.py:70
  33.8 2.3 %fusion.88 = (f32[256,2046]{0,1:T(8,128)}, f32[256,2046]{0,1:T(8,128)}) fusion(f32[256,2048]{0,1:T(8,128)S(1)} %bitcast.59), kind=kLoop, calls=%fused_computation.140 | loop fusion | bytes 8380416 | tf_op jit(solution)/shard_map/jit(_roll_static)/slice | solution.py:70
  36.1 2.3 %fusion.90 = (f32[256,2047]{0,1:T(8,128)}, f32[256,2047]{0,1:T(8,128)}) fusion(f32[256,2048]{0,1:T(8,128)S(1)} %bitcast.60), kind=kLoop, calls=%fused_computation.142 | loop fusion | bytes 8384512 | tf_op jit(solution)/shard_map/jit(_roll_static)/slice | solution.py:70
  38.4 2.3 %fusion.64 = (f32[256,2034]{0,1:T(8,128)}, f32[256,2034]{0,1:T(8,128)}) fusion(f32[256,2048]{0,1:T(8,128)S(1)} %bitcast.61), kind=kLoop, calls=%fused_computation.116 | loop fusion | bytes 8331264 | tf_op jit(solution)/shard_map/jit(_roll_static)/slice | solution.py:70
  40.7 2.3 %fusion.66 = (f32[256,2035]{0,1:T(8,128)}, f32[256,2035]{0,1:T(8,128)}) fusion(f32[256,2048]{0,1:T(8,128)S(1)} %bitcast.62), kind=kLoop, calls=%fused_computation.118 | loop fusion | bytes 8335360 | tf_op jit(solution)/shard_map/jit(_roll_static)/slice | solution.py:70
  43.0 2.3 %fusion.68 = (f32[256,2036]{0,1:T(8,128)}, f32[256,2036]{0,1:T(8,128)}) fusion(f32[256,2048]{0,1:T(8,128)S(1)} %bitcast.63), kind=kLoop, calls=%fused_computation.120 | loop fusion | bytes 8339456 | tf_op jit(solution)/shard_map/jit(_roll_static)/slice | solution.py:70
  45.3 2.3 %fusion.70 = (f32[256,2037]{0,1:T(8,128)}, f32[256,2037]{0,1:T(8,128)}) fusion(f32[256,2048]{0,1:T(8,128)S(1)} %bitcast.64), kind=kLoop, calls=%fused_computation.122 | loop fusion | bytes 8343552 | tf_op jit(solution)/shard_map/jit(_roll_static)/slice | solution.py:70
  47.6 2.3 %fusion.72 = (f32[256,2038]{0,1:T(8,128)}, f32[256,2038]{0,1:T(8,128)}) fusion(f32[256,2048]{0,1:T(8,128)S(1)} %bitcast.65), kind=kLoop, calls=%fused_computation.124 | loop fusion | bytes 8347648 | tf_op jit(solution)/shard_map/jit(_roll_static)/slice | solution.py:70
  49.9 2.3 %fusion.74 = (f32[256,2039]{0,1:T(8,128)}, f32[256,2039]{0,1:T(8,128)}) fusion(f32[256,2048]{0,1:T(8,128)S(1)} %bitcast.66), kind=kLoop, calls=%fused_computation.126 | loop fusion | bytes 8351744 | tf_op jit(solution)/shard_map/jit(_roll_static)/slice | solution.py:70
  52.1 2.2 %fusion.76 = (f32[256,2040]{0,1:T(8,128)}, f32[256,2040]{0,1:T(8,128)}) fusion(f32[256,2048]{0,1:T(8,128)S(1)} %bitcast.67), kind=kLoop, calls=%fused_computation.128 | loop fusion | bytes 8355840 | tf_op jit(solution)/shard_map/jit(_roll_static)/slice | solution.py:70
  54.3 2.3 %fusion.62 = (f32[256,2033]{0,1:T(8,128)}, f32[256,2033]{0,1:T(8,128)}) fusion(f32[256,2048]{0,1:T(8,128)S(1)} %bitcast.68), kind=kLoop, calls=%fused_computation.114 | loop fusion | bytes 8327168 | tf_op jit(solution)/shard_map/jit(_roll_static)/slice | solution.py:70
  56.8 27.9 %fusion.40 = f32[256,1024]{1,0:T(8,128)S(1)} fusion(bf16[2048,1024]{1,0:T(8,128)(2,1)} %constant.76.clone, f32[256,2038]{0,1:T(8,128)} %get-tuple-element.26, f32[256,10]{0,1:T(8,128)S(1)} %get-tuple-element.28, f32[256,2037]{0,1:T(8,128)} %get-tuple-element.22, f32[256,11]{0,1:T(8,128)S(1)} %get-tuple-element.24, f32[256,2036]{0,1:T(8,128)} %get-tuple-element.18, ...), kind=kOutput, calls=%fused_computation.76 | convolution fusion | flops 1121976320 | bytes 70254592 | tf_op jit(solution)/shard_map/dot_general | solution.py:89
  84.9 0.2 copy.22
  85.2 0.2 copy.23
  85.8 2.3 %collective-permute-start = (bf16[2,128,1024]{2,1,0:T(8,128)(2,1)S(1)}, bf16[2,128,1024]{2,1,0:T(8,128)(2,1)S(1)}, u32[]{:S(2)}, u32[]{:S(2)}) collective-permute-start(bf16[2,128,1024]{2,1,0:T(8,128)(2,1)S(1)} %get-tuple-element.67), channel_id=1, source_target_pairs={{0,4},{4,8},{8,12},{12,0},{1,5},{5,9},{9,13},{13,1},{2,6},{6,10},{... | collective-permute-start | bytes 1572872 | tf_op jit(solution)/shard_map/ppermute | solution.py:29
  88.1 16.9 %all_gather.3 = bf16[4,1,4,1]{2,3,1,0:T(2,128)(2,1)S(1)} all-gather(bf16[1,1,4,1]{2,3,1,0:T(2,128)(2,1)S(1)} %convert_element_type.56), channel_id=1, replica_groups=mesh['groups'=2,'chan'=4,'tm'=4] {'chan'}, dimensions={0}, use_global_device_ids=true | all-gather | bytes 40 | tf_op jit(solution)/shard_map/all_gather | solution.py:96
  105.0 0.2 convert_reduce_fusion
  105.3 0.5 collective-permute-start.2
  105.8 1.6 %collective-permute-start.1 = (bf16[2,128,1024]{2,1,0:T(8,128)(2,1)S(1)}, bf16[2,128,1024]{2,1,0:T(8,128)(2,1)S(1)}, u32[]{:S(2)}, u32[]{:S(2)}) collective-permute-start(bf16[2,128,1024]{2,1,0:T(8,128)(2,1)S(1)} %collective-permute-done), channel_id=1, source_target_pairs={{0,4},{4,8},{8,12},{12,0},{1,5},{5,9},{9,13},{13,1},{2,6},{6,10},{... | collective-permute-start | bytes 1572872 | tf_op jit(solution)/shard_map/ppermute | solution.py:29
  107.4 20.6 %collective-permute-done.2 = bf16[2,128,1024]{2,1,0:T(8,128)(2,1)S(1)} collective-permute-done((bf16[2,128,1024]{2,1,0:T(8,128)(2,1)S(1)}, bf16[2,128,1024]{2,1,0:T(8,128)(2,1)S(1)}, u32[]{:S(2)}, u32[]{:S(2)}) %collective-permute-start.2) | collective-permute-done | bytes 524320 | tf_op jit(solution)/shard_map/ppermute | solution.py:31
  128.0 1.2 pad_maximum_fusion
  129.3 2.0 %gather_fusion = bf16[4,2,128,1024]{3,2,1,0:T(8,128)(2,1)} fusion(bf16[4,2,128,1024]{3,2,1,0:T(8,128)(2,1)S(1)} %pad_maximum_fusion, s32[1024]{0:T(1024)S(1)} %pad_clamp_fusion.1), kind=kCustom, calls=%fused_computation | custom fusion | bytes 4194320 | tf_op jit(solution)/shard_map/gather | solution.py:34
  131.3 2.2 %gather_fusion.1 = bf16[4,128,1024]{2,1,0:T(8,128)(2,1)S(1)} fusion(bf16[8,128,1024]{2,1,0:T(8,128)(2,1)} %bitcast.85, s32[1024]{0:T(1024)S(1)} %pad_clamp_fusion), kind=kCustom, calls=%fused_computation.1 | custom fusion | bytes 2097168 | tf_op jit(solution)/shard_map/gather | solution.py:101
  133.5 0.7 fusion.34
  134.3 1.0 copy.27
  (36 shorter events, 0.7 us)
Async XLA Ops:
  85.4 2.7 %copy-start.1 = (s32[1,1,4,1]{2,3,1,0:T(1,128)S(1)}, s32[1,1,4,1]{2,3,1,0:T(1,128)}, u32[]{:S(2)}) copy-start(s32[1,1,4,1]{2,3,1,0:T(1,128)} %param.5) | copy-start | bytes 52
  85.4 22.0 %copy-start.2 = (s32[1,1,4]{2,1,0:T(1,128)S(1)}, s32[1,1,4]{2,1,0:T(1,128)}, u32[]{:S(2)}) copy-start(s32[1,1,4]{2,1,0:T(1,128)} %param.6) | copy-start | bytes 52
  85.8 20.0 %collective-permute-start = (bf16[2,128,1024]{2,1,0:T(8,128)(2,1)S(1)}, bf16[2,128,1024]{2,1,0:T(8,128)(2,1)S(1)}, u32[]{:S(2)}, u32[]{:S(2)}) collective-permute-start(bf16[2,128,1024]{2,1,0:T(8,128)(2,1)S(1)} %get-tuple-element.67), channel_id=1, source_target_pairs={{0,4},{4,8},{8,12},{12,0},{1,5},{5,9},{9,13},{13,1},{2,6},{6,10},{... | collective-permute-start | bytes 1572872 | tf_op jit(solution)/shard_map/ppermute | solution.py:29
  105.3 22.7 %collective-permute-start.2 = (bf16[2,128,1024]{2,1,0:T(8,128)(2,1)S(1)}, bf16[2,128,1024]{2,1,0:T(8,128)(2,1)S(1)}, u32[]{:S(2)}, u32[]{:S(2)}) collective-permute-start(bf16[2,128,1024]{2,1,0:T(8,128)(2,1)S(1)} %get-tuple-element.67), channel_id=1, source_target_pairs={{4,0},{8,4},{12,8},{0,12},{5,1},{9,5},{13,9},{1,13},{6,2},{10,6},{... | collective-permute-start | bytes 1572872 | tf_op jit(solution)/shard_map/ppermute | solution.py:31
  105.8 22.2 %copy-start = (bf16[2,128,1024]{2,1,0:T(8,128)(2,1)}, bf16[2,128,1024]{2,1,0:T(8,128)(2,1)S(1)}, u32[]{:S(2)}) copy-start(bf16[2,128,1024]{2,1,0:T(8,128)(2,1)S(1)} %collective-permute-done) | copy-start | bytes 1572868
  105.8 22.2 %collective-permute-start.1 = (bf16[2,128,1024]{2,1,0:T(8,128)(2,1)S(1)}, bf16[2,128,1024]{2,1,0:T(8,128)(2,1)S(1)}, u32[]{:S(2)}, u32[]{:S(2)}) collective-permute-start(bf16[2,128,1024]{2,1,0:T(8,128)(2,1)S(1)} %collective-permute-done), channel_id=1, source_target_pairs={{0,4},{4,8},{8,12},{12,0},{1,5},{5,9},{9,13},{13,1},{2,6},{6,10},{... | collective-permute-start | bytes 1572872 | tf_op jit(solution)/shard_map/ppermute | solution.py:29
